TPU v7x, 128 devices: a whole 4x4x4 slice. The times are simulated.
128 devices in a mesh: shard: 8 (over y, core), tensor: 4 (over z), section: 4 (over x).
Axes of the slice: x: 4, y: 4, z: 4, core: 2. Of those that a mesh axis runs over, the one named last changes fastest.
Arguments:
- activations: bfloat16 [4, 16384, 2048], P('section', 'shard'), may hold values from -500 to 500, as said below
- out_grad: bfloat16 [4, 16384, 8192], P('section', 'shard', 'tensor'), may hold values from -30 to 30, as said below
- basis: float32 [4, 2048, 256], P('section', 'shard'), may hold values from -0.125 to 0.125
- first_moment: float32 [4, 256, 8192], P('section', 'shard', 'tensor'), may hold values from -6 to 6
- second_moment: float32 [4, 256, 8192], P('section', 'shard', 'tensor'), may hold values from 0.5 to 2
- gain_partial: float32 [4, 8, 2048], P('section', 'shard'), may hold values from -4096 to 4096
- gain_first: float32 [4, 2048], P('section', 'shard'), may hold values from -6 to 6
- gain_second: float32 [4, 2048], P('section', 'shard'), may hold values from 0.5 to 2
Outputs:
- update: float32 [4, 2048, 8192], P('section', 'shard', 'tensor')
- first_out: float32 [4, 256, 8192], P('section', 'shard', 'tensor')
- second_out: float32 [4, 256, 8192], P('section', 'shard', 'tensor')
- new_basis: float32 [4, 2048, 256], P('section', ('shard', 'tensor'))
- gain_step: float32 [4, 2048], P('section', 'shard')
- gain_first_out: float32 [4, 2048], P('section', 'shard')
- gain_second_out: float32 [4, 2048], P('section', 'shard')
Inputs may be any that keep to these rules, and one draw needn't show every extreme that they name: Real-valued activations whose column scales differ from column to column. `out_grad`: Real-valued gradients whose column scales differ from column to column.
All inputs are finite; a program needn't handle non-finite values.
Results may differ from a plain program's by a relative error of at most 0.0003.
Values sent between devices are 32-bit elements; how exact they have to be, the bound alone decides.
No kernel may reach another device: no remote copies, remote signals or barrier semaphores. Data moves between devices by JAX's collectives and lax.ppermute only.
A program may use at most 128 MiB of HBM per device.

v0:
```python
import jax
import jax.numpy as jnp
from jax import lax
from jax.sharding import PartitionSpec as P

D = 2048
FF = 8192
NS_STEPS = 5
STEP = 8
exact_mode = lax.Precision.HIGHEST
beta_one = 0.9
beta_two = 0.999
adam_eps = 1e-08
clip_eps = 1e-06
ns_eps = 1e-07
coef_first = 3.4445
coef_second = -4.775
coef_third = 2.0315


def adam_direction(clipped, first_old, second_old):
    first_new = beta_one * first_old + (1.0 - beta_one) * clipped
    second_new = beta_two * second_old + (1.0 - beta_two) * clipped * clipped
    direction = (
        first_new
        / (1.0 - beta_one**STEP)
        / (jnp.sqrt(second_new / (1.0 - beta_two**STEP)) + adam_eps)
    )
    return (first_new, second_new, direction)


def ns_update(current, gram):
    mixer = coef_second * gram + coef_third * jnp.dot(gram, gram, precision=exact_mode)
    return coef_first * current + jnp.dot(current, mixer, precision=exact_mode)


def gram_of(block):
    local_gram = jnp.dot(block.T, block, precision=exact_mode)
    return lax.psum(local_gram, ("shard", "tensor"))


def shards(
    activations, out_grad, basis, first_moment, second_moment, gain_partial, gain_first, gain_second
):
    tensors = lax.axis_size("tensor")
    shard_pos = lax.axis_index("shard")
    layer_count = activations.shape[0]
    rows_here = basis.shape[1]
    rank_rows = first_moment.shape[1]
    cols_here = out_grad.shape[2]
    layer_index = 0
    tokens_in = activations[layer_index]
    grads_out = out_grad[layer_index]
    basis_here = basis[layer_index]

    def row_term(start, count, tokens_in=tokens_in, grads_out=grads_out):
        return lax.dot_general(
            tokens_in, grads_out, (((0,), (0,)), ((), ())), preferred_element_type=jnp.float32
        )

    grad_block = lax.psum_scatter(
        row_term(jnp.int32(0), lax.axis_size("shard") * rows_here),
        "shard",
        scatter_dimension=0,
        tiled=True,
    )
    part_proj = jnp.dot(basis_here.T, grad_block, precision=exact_mode)
    proj_full, gain_total = lax.psum((part_proj, gain_partial[layer_index, 0]), "shard")
    proj_rows = lax.dynamic_slice_in_dim(proj_full, shard_pos * rank_rows, rank_rows, 0)
    square_sum = jnp.sum(grad_block * grad_block)

    def refresh_term(start, count, grad_block=grad_block, proj_full=proj_full):
        return lax.dot_general(
            grad_block, proj_full, (((1,), (1,)), ((), ())), precision=exact_mode
        )

    refreshed = lax.psum_scatter(
        refresh_term(jnp.int32(0), lax.axis_size("tensor") * (rows_here // tensors)),
        "tensor",
        scatter_dimension=0,
        tiled=True,
    )
    kept_list = [basis_here]
    gain_own = lax.dynamic_slice_in_dim(gain_total, shard_pos * rows_here, rows_here, 0)
    square_sum = square_sum + jnp.sum(gain_own * gain_own) / float(tensors)
    proj_list = [proj_rows]
    gain_list = [gain_own]
    refresh_list = [refreshed]
    total_sq = lax.psum(square_sum, ("shard", "tensor", "section"))
    entry_count = float(lax.axis_size("section") * layer_count * (D * FF + D))
    clip = jnp.minimum(1.0, lax.rsqrt(total_sq / entry_count + clip_eps))
    layer_index = 0
    first_new, second_new, direction = adam_direction(
        clip * proj_list[layer_index], first_moment[layer_index], second_moment[layer_index]
    )
    firsts = [first_new]
    seconds = [second_new]
    kept_basis = kept_list[layer_index]

    def fold_rows(total, piece, start, kept_basis=kept_basis):
        return jnp.dot(kept_basis, piece, precision=exact_mode)

    empty = jnp.zeros((rows_here, cols_here), jnp.float32)
    update_here = fold_rows(
        empty, lax.all_gather(direction, "shard", axis=0, tiled=True), jnp.int32(0)
    )
    updates = [update_here]
    refreshed = refresh_list[layer_index]
    frob = lax.psum(jnp.sum(refreshed * refreshed), ("shard", "tensor"))
    current = refreshed / jnp.sqrt(frob + ns_eps)
    gram = gram_of(current)
    for step_index in range(NS_STEPS):
        current = ns_update(current, gram)
        if step_index + 1 < NS_STEPS:
            gram = gram_of(current)
    bases = [current]
    gain_first_new, gain_second_new, gain_dir = adam_direction(
        clip * gain_list[layer_index], gain_first[layer_index], gain_second[layer_index]
    )
    gain_steps = [gain_dir]
    gain_firsts = [gain_first_new]
    gain_seconds = [gain_second_new]
    return (
        jnp.stack(updates),
        jnp.stack(firsts),
        jnp.stack(seconds),
        jnp.stack(bases),
        jnp.stack(gain_steps),
        jnp.stack(gain_firsts),
        jnp.stack(gain_seconds),
    )


def solution(mesh):
    placed = (
        P("section", "shard", None),
        P("section", "shard", "tensor"),
        P("section", "shard", None),
        P("section", "shard", "tensor"),
        P("section", "shard", "tensor"),
        P("section", "shard", None),
        P("section", "shard"),
        P("section", "shard"),
    )
    return jax.shard_map(
        shards,
        mesh=mesh,
        in_specs=placed,
        out_specs=(
            P("section", "shard", "tensor"),
            P("section", "shard", "tensor"),
            P("section", "shard", "tensor"),
            P("section", ("shard", "tensor"), None),
            P("section", "shard"),
            P("section", "shard"),
            P("section", "shard"),
        ),
        check_vma=False,
    )
```

profile of v0, /device:TPU:1, one launch (start us, length us, event | category | flops | bytes accessed | tf_op | source)
XLA Modules:
  0.0 854.7 jit_solution(13370359571268590590)
XLA Ops:
  7.2 24.3 %fusion = f32[2048,2048]{1,0:T(8,128)} fusion(bf16[1,2048,2048]{2,1,0:T(8,128)(2,1)} %param.9, bf16[1,2048,2048]{2,1,0:T(8,128)(2,1)} %param.8), kind=kOutput, calls=%fused_computation | convolution fusion | flops 17179869184 | bytes 33554432 | tf_op jit(solution)/shard_map/dot_general | solution.py:57
  31.6 94.5 %reduce-scatter.3.cloned.1.call-done = f32[256,2048]{1,0:T(8,128)} async-done(((f32[2048,2048]{1,0:T(8,128)}), f32[256,2048]{1,0:T(8,128)}) %reduce-scatter.3.cloned.1.call-update) | async-done | bytes 2097168 | tf_op jit(solution)/shard_map/reduce_scatter | solution.py:61
  126.1 6.4 convolution_bitcast_fusion.1
  132.6 64.0 %all-reduce.7.cloned.1.call-done = f32[256,2048]{0,1:T(8,128)} async-done(((f32[256,2048]{0,1:T(8,128)}), f32[256,2048]{0,1:T(8,128)}) %all-reduce.7.cloned.1.call-update) | async-done | bytes 2097168 | tf_op jit(solution)/shard_map/psum | solution.py:68
  196.6 4.2 fusion.17
  200.9 20.4 %reduce-scatter.5.cloned.1.call-done = f32[64,256]{1,0:T(8,128)} async-done(((f32[256,256]{1,0:T(8,128)}), f32[64,256]{1,0:T(8,128)}) %reduce-scatter.5.cloned.1.call-update) | async-done | bytes 65552 | tf_op jit(solution)/shard_map/reduce_scatter | solution.py:77
  222.7 62.0 %psum.66 = f32[]{:T(128)} all-reduce(f32[]{:T(128)} %multiply_reduce_fusion.1), channel_id=1, replica_groups=mesh['shard'=8,'tensor'=4,'section'=4] {'shard','tensor'}, use_global_device_ids=true, to_apply=%region_8.0 | all-reduce | flops 1 | bytes 8 | tf_op jit(solution)/shard_map/psum | solution.py:109
  285.4 2.0 fusion.14
  287.5 104.3 %all-reduce.9.cloned.1.call-done = f32[256,256]{1,0:T(8,128)} async-done(((f32[256,256]{1,0:T(8,128)}), f32[256,256]{1,0:T(8,128)}) %all-reduce.9.cloned.1.call-update) | async-done | bytes 262160 | tf_op jit(solution)/shard_map/psum | solution.py:39
  395.8 101.9 %all-reduce.11.cloned.1.call-done = f32[256,256]{1,0:T(8,128)} async-done(((f32[256,256]{1,0:T(8,128)}), f32[256,256]{1,0:T(8,128)}) %all-reduce.11.cloned.1.call-update) | async-done | bytes 262160 | tf_op jit(solution)/shard_map/psum | solution.py:39
  501.9 2.3 copy.21
  504.2 13.5 %psum.63 = f32[2048]{0:T(1024)S(1)} all-reduce(f32[2048]{0:T(1024)S(1)} %bitcast.72), channel_id=1, replica_groups=mesh['shard'=8,'tensor'=4,'section'=4] {'shard'}, use_global_device_ids=true, to_apply=%region_2.0 | all-reduce | flops 2048 | bytes 16384 | tf_op jit(solution)/shard_map/psum | solution.py:68
  519.0 84.3 %all-reduce.13.cloned.1.call-done = f32[256,256]{1,0:T(8,128)} async-done(((f32[256,256]{1,0:T(8,128)}), f32[256,256]{1,0:T(8,128)}) %all-reduce.13.cloned.1.call-update) | async-done | bytes 262160 | tf_op jit(solution)/shard_map/psum | solution.py:39
  603.3 1.5 fusion.5
  608.2 65.9 %psum.64 = f32[]{:T(128)} all-reduce(f32[]{:T(128)S(6)} %add.92), channel_id=1, replica_groups=mesh['shard'=8,'tensor'=4,'section'=4] {'shard','tensor','section'}, use_global_device_ids=true, to_apply=%region_4.0 | all-reduce | flops 1 | bytes 8 | tf_op jit(solution)/shard_map/psum | solution.py:89
  674.7 34.5 %all-reduce.15.cloned.1.call-done = f32[256,256]{1,0:T(8,128)} async-done(((f32[256,256]{1,0:T(8,128)}), f32[256,256]{1,0:T(8,128)}) %all-reduce.15.cloned.1.call-update) | async-done | bytes 262160 | tf_op jit(solution)/shard_map/psum | solution.py:39
  709.2 1.5 fusion.4
  712.2 3.3 fusion.13
  715.5 2.3 copy.22
  720.6 93.8 %all-reduce.17.cloned.1.call-done = f32[256,256]{1,0:T(8,128)} async-done(((f32[256,256]{1,0:T(8,128)}), f32[256,256]{1,0:T(8,128)}) %all-reduce.17.cloned.1.call-update) | async-done | bytes 262160 | tf_op jit(solution)/shard_map/psum | solution.py:39
  814.4 1.5 fusion.3
  816.9 24.5 %all-gather.2.cloned.1.call-done = f32[256,2048]{1,0:T(8,128)} async-done(((f32[32,2048]{1,0:T(8,128)}), f32[256,2048]{1,0:T(8,128)}) %all-gather.2.cloned.1.call-update) | async-done | bytes 2097168 | tf_op jit(solution)/shard_map/all_gather | solution.py:105
  841.4 5.0 convolution_bitcast_fusion
  846.4 1.8 copy.23
  (52 shorter events, 18.2 us)
Async XLA Ops:
  7.2 119.0 %copy-start = (f32[1,256,256]{2,1,0:T(8,128)S(1)}, f32[1,256,256]{2,1,0:T(8,128)}, u32[]{:S(2)}) copy-start(f32[1,256,256]{2,1,0:T(8,128)} %param.10) | copy-start | bytes 786436
  7.2 119.0 %reduce-scatter.3.cloned.1.call-start = ((), (), s32[]{:S(2)}) async-start(), calls=%async_computation.2 | async-start | bytes 18874368 | tf_op jit(solution)/shard_map/reduce_scatter | solution.py:61
  31.5 165.1 %all-reduce.7.cloned.1.call-start = ((), (), s32[]{:S(2)}) async-start(), calls=%async_computation.3 | async-start | bytes 4194304 | tf_op jit(solution)/shard_map/psum | solution.py:68
  132.5 64.1 %copy-start.1 = (f32[256,2048]{1,0:T(8,128)S(1)}, f32[256,2048]{1,0:T(8,128)}, u32[]{:S(2)}) copy-start(f32[256,2048]{1,0:T(8,128)} %reduce-scatter.3.cloned.1.call-done) | copy-start | bytes 6291460
  132.5 88.7 %reduce-scatter.5.cloned.1.call-start = ((), (), s32[]{:S(2)}) async-start(), calls=%async_computation.5 | async-start | bytes 327680 | tf_op jit(solution)/shard_map/reduce_scatter | solution.py:77
  200.8 191.0 %all-reduce.9.cloned.1.call-start = ((), (), s32[]{:S(2)}) async-start(), calls=%async_computation.6 | async-start | bytes 524288 | tf_op jit(solution)/shard_map/psum | solution.py:39
  287.4 210.3 %all-reduce.11.cloned.1.call-start = ((), (), s32[]{:S(2)}) async-start(), calls=%async_computation.7 | async-start | bytes 524288 | tf_op jit(solution)/shard_map/psum | solution.py:39
  395.6 108.6 %copy-start.4 = (f32[1,1,2048]{2,1,0:T(1,128)S(1)}, f32[1,1,2048]{2,1,0:T(1,128)}, u32[]{:S(2)}) copy-start(f32[1,1,2048]{2,1,0:T(1,128)} %param.13) | copy-start | bytes 24580
  395.6 207.8 %all-reduce.13.cloned.1.call-start = ((), (), s32[]{:S(2)}) async-start(), calls=%async_computation.8 | async-start | bytes 524288 | tf_op jit(solution)/shard_map/psum | solution.py:39
  500.6 208.6 %all-reduce.15.cloned.1.call-start = ((), (), s32[]{:S(2)}) async-start(), calls=%async_computation.9 | async-start | bytes 524288 | tf_op jit(solution)/shard_map/psum | solution.py:39
  606.2 208.2 %all-reduce.17.cloned.1.call-start = ((), (), s32[]{:S(2)}) async-start(), calls=%async_computation.10 | async-start | bytes 524288 | tf_op jit(solution)/shard_map/psum | solution.py:39
  607.4 104.8 %copy-start.2 = (f32[1,32,2048]{1,2,0:T(8,128)S(1)}, f32[1,32,2048]{1,2,0:T(8,128)}, u32[]{:S(2)}) copy-start(f32[1,32,2048]{1,2,0:T(8,128)} %copy.21) | copy-start | bytes 786436
  712.1 5.7 copy-start.5
  712.1 5.8 copy-start.6
  712.1 129.2 %all-gather.2.cloned.1.call-start = ((), (), s32[]{:S(2)}) async-start(), calls=%async_computation.4 | async-start | bytes 2359296 | tf_op jit(solution)/shard_map/all_gather | solution.py:105
  715.5 3.1 copy-start.3
Sparse Core Ops, SparseCore 0:
  31.7 94.4 reduce-scatter.2
  132.6 63.9 all-reduce.6
  200.9 20.2 reduce-scatter.4
  287.6 104.1 all-reduce.8
  395.7 101.9 all-reduce.10
  501.4 101.9 all-reduce.12
  607.1 102.0 all-reduce.14
  712.4 101.9 all-reduce.16
  816.2 25.1 all-gather.1
where the time goes:
time: 855 us
  waiting for transfers between devices  622 us (73%)
  blocking collectives  141 us (16%)
  matrix products  56.7 us (7%)
  between operations  16.8 us (2%)
  local copies, waits for them, and re-layouts  9.74 us (1%)
    psum x5, waiting for transfers between devices, gram_of(): return lax.psum(local_gram, ('shard', 'tensor'))  419 us
    reduce_scatter x1, waiting for transfers between devices, shards(): lax.psum_scatter(row_term(jnp.int32(0), lax.axis_size('shard') * rows_her...  94.5 us
    psum x1, blocking collectives, shards(): total_sq = lax.psum(square_sum, ('shard', 'tensor', 'section'))  65.9 us
    psum x1, waiting for transfers between devices, shards(): lax.psum((part_proj, gain_partial[layer_index, 0]), 'shard')  64 us
    psum x1, blocking collectives, shards(): frob = lax.psum(jnp.sum(refreshed * refreshed), ('shard', 'tensor'))  62 us
    all_gather x1, waiting for transfers between devices, shards(): lax.all_gather(direction, 'shard', axis=0, tiled=True)  24.5 us
    dot_general x1, matrix products, row_term(): lax.dot_general(tokens_in, grads_out, (((0,), (0,)), ((), ())), preferred...  24.3 us
    reduce_scatter x1, waiting for transfers between devices, shards(): lax.psum_scatter(refresh_term(jnp.int32(0), lax.axis_size('tensor') * (ro...  20.4 us
  transfers between devices with their start and end apart: 9, of which 9 were waited for; matrix products, arithmetic and copies ran while one was open for 2% of the time, Pallas kernels for 0%

commit v1 on v0

--- a/solution.py
+++ b/solution.py
@@ -16,6 +16,22 @@
 coef_first = 3.4445
 coef_second = -4.775
 coef_third = 2.0315
+
+
+def ring_gather(x, axis, dim):
+    ways, here, turn = (lax.axis_size(axis), lax.axis_index(axis), x.shape[dim])
+    shape = [n * ways if d == dim else n for d, n in enumerate(x.shape)]
+    full = lax.dynamic_update_slice_in_dim(jnp.zeros(shape, x.dtype), x, here * turn, axis=dim)
+    going_up = going_down = x
+    for far in range(1, ways // 2 + 1):
+        going_up = lax.ppermute(going_up, axis, [(d, (d + 1) % ways) for d in range(ways)])
+        full = lax.dynamic_update_slice_in_dim(full, going_up, (here - far) % ways * turn, axis=dim)
+        if 2 * far < ways:
+            going_down = lax.ppermute(going_down, axis, [(d, (d - 1) % ways) for d in range(ways)])
+            full = lax.dynamic_update_slice_in_dim(
+                full, going_down, (here + far) % ways * turn, axis=dim
+            )
+    return full
 
 
 def adam_direction(clipped, first_old, second_old):
@@ -101,9 +117,7 @@
         return jnp.dot(kept_basis, piece, precision=exact_mode)
 
     empty = jnp.zeros((rows_here, cols_here), jnp.float32)
-    update_here = fold_rows(
-        empty, lax.all_gather(direction, "shard", axis=0, tiled=True), jnp.int32(0)
-    )
+    update_here = fold_rows(empty, ring_gather(direction, "shard", 0), jnp.int32(0))
     updates = [update_here]
     refreshed = refresh_list[layer_index]
     frob = lax.psum(jnp.sum(refreshed * refreshed), ("shard", "tensor"))

time: 855 us -> 888 us (1.039)
  local copies, waits for them, and re-layouts: 9.74 us -> 79.7 us
  waiting for transfers between devices: 622 us -> 578 us
    dynamic_update_slice x0 -> x8, local copies, waits for them, and re-layouts: none -> 59.4 us  [the longest x4 26.2 us: ring_gather(): lax.dynamic_update_slice_in_dim(full, going_up, (here - far) % ways * tur...]
    all_gather x1 -> x0, waiting for transfers between devices: 24.5 us -> none  [shards(): lax.all_gather(direction, 'shard', axis=0, tiled=True)]
    reduce_scatter x1, waiting for transfers between devices: 20.4 us -> 0.02 us  [shards(): lax.psum_scatter(refresh_term(jnp.int32(0), lax.axis_size('tensor') * (ro...]
    ppermute x0 -> x7, local copies, waits for them, and re-layouts: none -> 8.95 us  [the longest x4 5.11 us: ring_gather(): lax.ppermute(going_up, axis, [(d, (d + 1) % ways) for d in range(ways)])]
  transfers between devices with their start and end apart: 9 -> 15, of which waited for: 9 -> 7; matrix products, arithmetic and copies ran while one was open for 2% -> 11% of each run, Pallas kernels for 0% -> 0%
where the time goes in v1:
time: 888 us; the launch traced here: 887 us
  waiting for transfers between devices  578 us (65%)
  blocking collectives  142 us (16%)
  local copies, waits for them, and re-layouts  79.7 us (9%)
  matrix products  54.1 us (6%)
  between operations  17.3 us (2%)
    psum x5, waiting for transfers between devices, gram_of(): return lax.psum(local_gram, ('shard', 'tensor'))  419 us
    reduce_scatter x1, waiting for transfers between devices, shards(): lax.psum_scatter(row_term(jnp.int32(0), lax.axis_size('shard') * rows_her...  94.5 us
    psum x1, blocking collectives, shards(): total_sq = lax.psum(square_sum, ('shard', 'tensor', 'section'))  66 us
    psum x1, waiting for transfers between devices, shards(): lax.psum((part_proj, gain_partial[layer_index, 0]), 'shard')  64 us
    psum x1, blocking collectives, shards(): frob = lax.psum(jnp.sum(refreshed * refreshed), ('shard', 'tensor'))  61.2 us
    dynamic_update_slice x4, local copies, waits for them, and re-layouts, ring_gather(): lax.dynamic_update_slice_in_dim(full, going_up, (here - far) % ways * tur...  26.2 us
    dot_general x1, matrix products, row_term(): lax.dot_general(tokens_in, grads_out, (((0,), (0,)), ((), ())), preferred...  24.3 us
    dynamic_update_slice x3, local copies, waits for them, and re-layouts, ring_gather(): lax.dynamic_update_slice_in_dim(full, going_down, (here + far) % ways * t...  23.6 us
  transfers between devices with their start and end apart: 15, of which 7 were waited for; matrix products, arithmetic and copies ran while one was open for 11% of the time, Pallas kernels for 0%

profile of v1, /device:TPU:1, one launch (start us, length us, event | category | flops | bytes accessed | tf_op | source)
XLA Modules:
  0.0 887.1 jit_solution(4836384813311363831)
XLA Ops:
  7.2 24.3 %fusion = f32[2048,2048]{1,0:T(8,128)} fusion(bf16[1,2048,2048]{2,1,0:T(8,128)(2,1)} %param.9, bf16[1,2048,2048]{2,1,0:T(8,128)(2,1)} %param.8), kind=kOutput, calls=%fused_computation | convolution fusion | flops 17179869184 | bytes 33554432 | tf_op jit(solution)/shard_map/dot_general | solution.py:73
  31.6 94.5 %reduce-scatter.3.cloned.1.call-done = f32[256,2048]{1,0:T(8,128)} async-done(((f32[2048,2048]{1,0:T(8,128)}), f32[256,2048]{1,0:T(8,128)}) %reduce-scatter.3.cloned.1.call-update) | async-done | bytes 2097168 | tf_op jit(solution)/shard_map/reduce_scatter | solution.py:77
  126.1 6.4 convolution_bitcast_fusion.1
  132.6 64.0 %all-reduce.7.cloned.1.call-done = f32[256,2048]{0,1:T(8,128)} async-done(((f32[256,2048]{0,1:T(8,128)}), f32[256,2048]{0,1:T(8,128)}) %all-reduce.7.cloned.1.call-update) | async-done | bytes 2097168 | tf_op jit(solution)/shard_map/psum | solution.py:84
  196.6 4.2 fusion.17
  204.5 14.5 %psum.63 = f32[2048]{0:T(1024)S(1)} all-reduce(f32[2048]{0:T(1024)S(1)} %bitcast.72), channel_id=1, replica_groups=mesh['shard'=8,'tensor'=4,'section'=4] {'shard'}, use_global_device_ids=true, to_apply=%region_2.0 | all-reduce | flops 2048 | bytes 16384 | tf_op jit(solution)/shard_map/psum | solution.py:84
  222.2 66.0 %psum.64 = f32[]{:T(128)} all-reduce(f32[]{:T(128)S(6)} %add.149), channel_id=1, replica_groups=mesh['shard'=8,'tensor'=4,'section'=4] {'shard','tensor','section'}, use_global_device_ids=true, to_apply=%region_4.0 | all-reduce | flops 1 | bytes 8 | tf_op jit(solution)/shard_map/psum | solution.py:105
  290.5 61.2 %psum.66 = f32[]{:T(128)} all-reduce(f32[]{:T(128)} %multiply_reduce_fusion.1), channel_id=1, replica_groups=mesh['shard'=8,'tensor'=4,'section'=4] {'shard','tensor'}, use_global_device_ids=true, to_apply=%region_8.9 | all-reduce | flops 1 | bytes 8 | tf_op jit(solution)/shard_map/psum | solution.py:123
  354.5 3.6 fusion.13
  358.4 5.0 collective-permute-start.1
  363.4 92.7 %all-reduce.9.cloned.1.call-done = f32[256,256]{1,0:T(8,128)} async-done(((f32[256,256]{1,0:T(8,128)}), f32[256,256]{1,0:T(8,128)}) %all-reduce.9.cloned.1.call-update) | async-done | bytes 262160 | tf_op jit(solution)/shard_map/psum | solution.py:55
  460.4 101.4 %all-reduce.11.cloned.1.call-done = f32[256,256]{1,0:T(8,128)} async-done(((f32[256,256]{1,0:T(8,128)}), f32[256,256]{1,0:T(8,128)}) %all-reduce.11.cloned.1.call-update) | async-done | bytes 262160 | tf_op jit(solution)/shard_map/psum | solution.py:55
  565.9 101.5 %all-reduce.13.cloned.1.call-done = f32[256,256]{1,0:T(8,128)} async-done(((f32[256,256]{1,0:T(8,128)}), f32[256,256]{1,0:T(8,128)}) %all-reduce.13.cloned.1.call-update) | async-done | bytes 262160 | tf_op jit(solution)/shard_map/psum | solution.py:55
  671.3 9.5 %dynamic_update_slice.24 = f32[256,2048]{0,1:T(8,128)S(1)} dynamic-update-slice(f32[256,2048]{0,1:T(8,128)S(1)} %broadcast_in_dim.3, f32[32,2048]{0,1:T(8,128)S(1)} %get-tuple-element.25, s32[]{:T(128)S(6)} %select_n.60, s32[]{:T(128)} %constant.85.clone.1) | dynamic-update-slice | bytes 524292 | tf_op jit(solution)/shard_map/dynamic_update_slice | solution.py:24
  686.6 8.0 dynamic_update_slice.25
  695.9 9.5 %dynamic_update_slice.26 = f32[256,2048]{0,1:T(8,128)S(1)} dynamic-update-slice(f32[256,2048]{0,1:T(8,128)S(1)} %dynamic_update_slice.25, f32[32,2048]{0,1:T(8,128)S(1)} %copy.25, s32[]{:T(128)S(6)} %select_n.64, s32[]{:T(128)} %constant.85.clone.1) | dynamic-update-slice | bytes 524292 | tf_op jit(solution)/shard_map/dynamic_update_slice | solution.py:31
  706.7 6.1 dynamic_update_slice.27
  714.1 9.5 %dynamic_update_slice.28 = f32[256,2048]{0,1:T(8,128)S(1)} dynamic-update-slice(f32[256,2048]{0,1:T(8,128)S(1)} %dynamic_update_slice.27, f32[32,2048]{0,1:T(8,128)S(1)} %copy.27, s32[]{:T(128)S(6)} %select_n.68, s32[]{:T(128)} %constant.85.clone.1) | dynamic-update-slice | bytes 524292 | tf_op jit(solution)/shard_map/dynamic_update_slice | solution.py:31
  724.9 6.1 dynamic_update_slice.29
  732.3 4.5 dynamic_update_slice.30
  738.0 34.6 %all-reduce.15.cloned.1.call-done = f32[256,256]{1,0:T(8,128)} async-done(((f32[256,256]{1,0:T(8,128)}), f32[256,256]{1,0:T(8,128)}) %all-reduce.15.cloned.1.call-update) | async-done | bytes 262160 | tf_op jit(solution)/shard_map/psum | solution.py:55
  776.9 6.1 dynamic_update_slice.31
  783.0 3.2 convolution_bitcast_fusion
  789.1 88.8 %all-reduce.17.cloned.1.call-done = f32[256,256]{1,0:T(8,128)} async-done(((f32[256,256]{1,0:T(8,128)}), f32[256,256]{1,0:T(8,128)}) %all-reduce.17.cloned.1.call-update) | async-done | bytes 262160 | tf_op jit(solution)/shard_map/psum | solution.py:55
  (81 shorter events, 44.4 us)
Async XLA Ops:
  7.2 119.0 %copy-start = (f32[1,256,256]{2,1,0:T(8,128)S(1)}, f32[1,256,256]{2,1,0:T(8,128)}, u32[]{:S(2)}) copy-start(f32[1,256,256]{2,1,0:T(8,128)} %param.10) | copy-start | bytes 786436
  7.2 119.0 %reduce-scatter.3.cloned.1.call-start = ((), (), s32[]{:S(2)}) async-start(), calls=%async_computation.2 | async-start | bytes 18874368 | tf_op jit(solution)/shard_map/reduce_scatter | solution.py:77
  31.5 165.1 %all-reduce.7.cloned.1.call-start = ((), (), s32[]{:S(2)}) async-start(), calls=%async_computation.3 | async-start | bytes 4194304 | tf_op jit(solution)/shard_map/psum | solution.py:84
  132.5 64.1 %copy-start.1 = (f32[256,2048]{1,0:T(8,128)S(1)}, f32[256,2048]{1,0:T(8,128)}, u32[]{:S(2)}) copy-start(f32[256,2048]{1,0:T(8,128)} %reduce-scatter.3.cloned.1.call-done) | copy-start | bytes 6291460
  132.5 156.5 %reduce-scatter.5.cloned.1.call-start = ((), (), s32[]{:S(2)}) async-start(), calls=%async_computation.4 | async-start | bytes 327680 | tf_op jit(solution)/shard_map/reduce_scatter | solution.py:93
  200.8 3.8 copy-start.5
  200.8 255.3 %all-reduce.9.cloned.1.call-start = ((), (), s32[]{:S(2)}) async-start(), calls=%async_computation.5 | async-start | bytes 524288 | tf_op jit(solution)/shard_map/psum | solution.py:55
  354.4 207.4 %all-reduce.11.cloned.1.call-start = ((), (), s32[]{:S(2)}) async-start(), calls=%async_computation.6 | async-start | bytes 524288 | tf_op jit(solution)/shard_map/psum | solution.py:55
  358.1 99.6 %copy-start.4 = (f32[64,256]{1,0:T(8,128)S(1)}, f32[64,256]{1,0:T(8,128)}, u32[]{:S(2)}) copy-start(f32[64,256]{1,0:T(8,128)} %reduce-scatter.5.cloned.1.call-done) | copy-start | bytes 196612
  358.1 101.1 %copy-start.6 = (f32[1,256]{1,0:T(1,128)S(1)}, f32[1,256]{1,0:T(1,128)}, u32[]{:S(2)}) copy-start(f32[1,256]{1,0:T(1,128)} %param.14) | copy-start | bytes 3076
  358.4 206.3 %copy-start.7 = (f32[1,256]{1,0:T(1,128)S(1)}, f32[1,256]{1,0:T(1,128)}, u32[]{:S(2)}) copy-start(f32[1,256]{1,0:T(1,128)} %param.15) | copy-start | bytes 3076
  358.4 100.8 %collective-permute-start = (f32[32,2048]{1,0:T(8,128)S(1)}, f32[32,2048]{1,0:T(8,128)S(1)}, u32[]{:S(2)}, u32[]{:S(2)}) collective-permute-start(f32[32,2048]{1,0:T(8,128)S(1)} %copy.22), channel_id=1, source_target_pairs={{0,16},{16,32},{32,48},{48,64},{64,80},{80,96},{96,112},{112,0},{1... | collective-permute-start | bytes 786440 | tf_op jit(solution)/shard_map/ppermute | solution.py:27
  358.4 101.9 %collective-permute-start.1 = (f32[32,2048]{1,0:T(8,128)S(1)}, f32[32,2048]{1,0:T(8,128)S(1)}, u32[]{:S(2)}, u32[]{:S(2)}) collective-permute-start(f32[32,2048]{1,0:T(8,128)S(1)} %copy.22), channel_id=1, source_target_pairs={{0,112},{16,0},{32,16},{48,32},{64,48},{80,64},{96,80},{112,96},{1... | collective-permute-start | bytes 786440 | tf_op jit(solution)/shard_map/ppermute | solution.py:30
  459.1 208.3 %all-reduce.13.cloned.1.call-start = ((), (), s32[]{:S(2)}) async-start(), calls=%async_computation.7 | async-start | bytes 524288 | tf_op jit(solution)/shard_map/psum | solution.py:55
  459.2 211.3 %copy-start.3 = (f32[32,2048]{1,0:T(8,128)}, f32[32,2048]{1,0:T(8,128)S(1)}, u32[]{:S(2)}) copy-start(f32[32,2048]{1,0:T(8,128)S(1)} %collective-permute-done) | copy-start | bytes 786436
  459.2 105.6 %collective-permute-start.2 = (f32[32,2048]{1,0:T(8,128)S(1)}, f32[32,2048]{1,0:T(8,128)}, u32[]{:S(2)}, u32[]{:S(2)}) collective-permute-start(f32[32,2048]{1,0:T(8,128)S(1)} %collective-permute-done), channel_id=1, source_target_pairs={{0,16},{16,32},{32,48},{48,64},{64,80},{80,96},{96,112},{112,0},{1... | collective-permute-start | bytes 786440 | tf_op jit(solution)/shard_map/ppermute | solution.py:27
  460.4 210.1 %copy-start.2 = (f32[32,2048]{1,0:T(8,128)}, f32[32,2048]{1,0:T(8,128)S(1)}, u32[]{:S(2)}) copy-start(f32[32,2048]{1,0:T(8,128)S(1)} %collective-permute-done.1) | copy-start | bytes 786436
  460.4 105.6 %collective-permute-start.3 = (f32[32,2048]{1,0:T(8,128)S(1)}, f32[32,2048]{1,0:T(8,128)}, u32[]{:S(2)}, u32[]{:S(2)}) collective-permute-start(f32[32,2048]{1,0:T(8,128)S(1)} %collective-permute-done.1), channel_id=1, source_target_pairs={{0,112},{16,0},{32,16},{48,32},{64,48},{80,64},{96,80},{112,96},{1... | collective-permute-start | bytes 786440 | tf_op jit(solution)/shard_map/ppermute | solution.py:30
  564.7 207.9 %all-reduce.15.cloned.1.call-start = ((), (), s32[]{:S(2)}) async-start(), calls=%async_computation.8 | async-start | bytes 524288 | tf_op jit(solution)/shard_map/psum | solution.py:55
  564.8 158.9 %collective-permute-start.4 = (f32[32,2048]{1,0:T(8,128)}, f32[32,2048]{1,0:T(8,128)}, u32[]{:S(2)}, u32[]{:S(2)}) collective-permute-start(f32[32,2048]{1,0:T(8,128)} %collective-permute-done.2), channel_id=1, source_target_pairs={{0,16},{16,32},{32,48},{48,64},{64,80},{80,96},{96,112},{112,0},{1... | collective-permute-start | bytes 786440 | tf_op jit(solution)/shard_map/ppermute | solution.py:27
  565.9 165.1 %collective-permute-start.5 = (f32[32,2048]{1,0:T(8,128)}, f32[32,2048]{1,0:T(8,128)}, u32[]{:S(2)}, u32[]{:S(2)}) collective-permute-start(f32[32,2048]{1,0:T(8,128)} %collective-permute-done.3), channel_id=1, source_target_pairs={{0,112},{16,0},{32,16},{48,32},{64,48},{80,64},{96,80},{112,96},{1... | collective-permute-start | bytes 786440 | tf_op jit(solution)/shard_map/ppermute | solution.py:30
  670.4 207.5 %all-reduce.17.cloned.1.call-start = ((), (), s32[]{:S(2)}) async-start(), calls=%async_computation.9 | async-start | bytes 524288 | tf_op jit(solution)/shard_map/psum | solution.py:55
  736.9 38.7 %collective-permute-start.6 = (f32[32,2048]{1,0:T(8,128)}, f32[32,2048]{1,0:T(8,128)}, u32[]{:S(2)}, u32[]{:S(2)}) collective-permute-start(f32[32,2048]{1,0:T(8,128)} %collective-permute-done.4), channel_id=1, source_target_pairs={{0,16},{16,32},{32,48},{48,64},{64,80},{80,96},{96,112},{112,0},{1... | collective-permute-start | bytes 786440 | tf_op jit(solution)/shard_map/ppermute | solution.py:27
Sparse Core Ops, SparseCore 0:
  31.7 94.4 reduce-scatter.2
  132.6 63.9 all-reduce.6
  200.9 20.3 reduce-scatter.4
  354.5 101.5 all-reduce.8
  459.8 101.9 all-reduce.10
  565.4 101.9 all-reduce.12
  670.6 101.9 all-reduce.14
  775.9 101.9 all-reduce.16
